TPU v7x, 32 devices: a whole 2x2x4 slice. The times are simulated.
32 devices in a mesh: groups: 2 (over y), range: 8 (over z, x), chan: 2 (over core).
Axes of the slice: x: 2, y: 2, z: 4, core: 2. Of those that a mesh axis runs over, the one named last changes fastest.
Arguments:
- echoes: bfloat16 [4, 512, 8, 1024], P('groups', 'chan', None, 'range'), parts along dimension 0, may hold values from -6 to 6
- chirp: float32 [2, 2049], replicated, may hold values from -0.09375 to 0.09375
- gates: int32 [4, 8], P('groups'), parts along dimension 0, may hold values from 0 to 1023, as said below
Outputs:
- compressed: bfloat16 [4, 512, 8, 1024], P('groups', 'chan', None, 'range'), parts along dimension 0
- covariance: float32 [4, 2, 2048, 4096], P('groups', 'chan', 'range'), parts along dimension 0
There are 2 independent parts, one for each index of `groups`. A program takes and returns all parts, laid end to end along the dimension named above; an argument that names none is the same for every part. Nothing has to cross between parts.
Inputs may be any that keep to these rules, and one draw needn't show every extreme that they name: `gates`: the 8 intervals are given in increasing order, do not intersect, lie within the 1024 cells, each holds one cell or more, and their lengths add up to 128. The first interval starts at cell 0, and the last is the single cell 1024 - 1.
All inputs are finite; a program needn't handle non-finite values.
Results may differ from a plain program's by a relative error of at most 0.0035.
Values may be sent and summed in bfloat16 or wider, within the bound.
No kernel may reach another device: no remote copies, remote signals or barrier semaphores. Data moves between devices by JAX's collectives and lax.ppermute only.
A program may use at most 128 MiB of HBM per device.

v0:
```python
from functools import partial
import math
import jax
import jax.numpy as jnp
from jax import lax
from jax.sharding import PartitionSpec as P

TRAIN = 128


def partner_2(value, axis, bit):
    mask = 2**bit
    pairs = [(source, source ^ mask) for source in range(lax.axis_size(axis))]
    return lax.ppermute(value, axis, pairs)


def as_sent(x):

    def short(part):
        return part.astype(jnp.bfloat16) if part.dtype == jnp.float32 else part

    return jax.tree.map(short, x)


def train_cells(gates, count):
    starts = gates[0]
    widths = gates[1]
    ends = jnp.cumsum(widths)
    places = jnp.arange(count, dtype=jnp.int32)
    which = jnp.sum((ends[None, :] <= places[:, None]).astype(jnp.int32), axis=1)
    onehot = jnp.arange(gates.shape[1], dtype=jnp.int32)[None, :] == which[:, None]
    offset = jnp.sum(jnp.where(onehot, (starts - (ends - widths))[None, :], 0), axis=1)
    return offset + places


def angle_tables(radix, nfft, sign):
    steps = jnp.arange(radix, dtype=jnp.int32)
    square = steps[:, None] * steps[None, :]
    small = sign * 2.0 * math.pi * (square % radix).astype(jnp.float32) / radix
    large = sign * 2.0 * math.pi * square.astype(jnp.float32) / nfft
    small_cos = jnp.cos(small)
    small_sin = jnp.sin(small)
    stacked = jnp.stack([small_cos, small_sin])
    block = jnp.concatenate(
        [
            jnp.concatenate([small_cos, small_sin], axis=1),
            jnp.concatenate([-small_sin, small_cos], axis=1),
        ],
        axis=0,
    )
    twiddle = jnp.concatenate([jnp.cos(large), jnp.sin(large)], axis=1)
    return (stacked, block, twiddle)


def merged_times(first, second):
    half = first.shape[-1] // 2
    first_re = first[..., :half]
    first_im = first[..., half:]
    second_re = second[..., :half]
    second_im = second[..., half:]
    return jnp.concatenate(
        [first_re * second_re - first_im * second_im, first_re * second_im + first_im * second_re],
        axis=-1,
    )


def left_section(stacked, values):
    mixed = jnp.einsum("ckn,...nr->...ckr", stacked, values, precision=lax.Precision.HIGHEST)
    half = values.shape[-1] // 2
    real_part = mixed[..., 0, :, :half] - mixed[..., 1, :, half:]
    imag_part = mixed[..., 1, :, :half] + mixed[..., 0, :, half:]
    return jnp.concatenate([real_part, imag_part], axis=-1)


def right_section(values, block):
    return jnp.einsum("...km,mj->...kj", values, block, precision=lax.Precision.HIGHEST)


def forward_dft(values, tables):
    stacked, block, twiddle = tables
    section = left_section(stacked, values)
    section = merged_times(section, twiddle)
    return right_section(section, block)


def inverse_upper(spectrum, tables):
    stacked, block, twiddle = tables
    section = right_section(spectrum, block)
    section = merged_times(section, twiddle)
    half = stacked.shape[1] // 2
    return left_section(stacked[:, half:], section)


def gram(left, right):
    contract = partial(
        lax.dot_general,
        dimension_numbers=(((1,), (1,)), ((), ())),
        preferred_element_type=jnp.float32,
    )
    real_part = contract(left[0], right[0]) + contract(left[1], right[1])
    imag_part = contract(left[1], right[0]) - contract(left[0], right[1])
    return jnp.stack([real_part, imag_part])


def on_device(echoes, chirp, gates):
    chans = echoes.shape[1]
    pulses = echoes.shape[2]
    cells_dev = echoes.shape[3]
    taps = chirp.shape[1]
    newlen = taps - 1
    nfft = 2 * newlen
    radix = math.isqrt(nfft)
    ranks = lax.axis_size("range")
    range_len = cells_dev * ranks
    nseg = (range_len + newlen - 1) // newlen
    forward_tables = angle_tables(radix, nfft, -1.0)
    inverse_tables = angle_tables(radix, nfft, 1.0)
    padded_taps = jnp.pad(chirp, ((0, 0), (0, nfft - taps))).reshape(2, radix, radix)
    response = forward_dft(
        jnp.concatenate([padded_taps[0], padded_taps[1]], axis=-1), forward_tables
    )
    series_total = chans * pulses
    local = echoes.reshape(2, series_total, cells_dev)
    cells = train_cells(gates, TRAIN)
    series_all = lax.all_to_all(local, "range", split_axis=1, concat_axis=2, tiled=True)
    values = series_all.astype(jnp.float32)
    count = values.shape[1]
    padded = jnp.pad(values, ((0, 0), (0, 0), (newlen, nseg * newlen - range_len)))
    blocks = padded.reshape(2, count, nseg + 1, newlen)
    frames = jnp.concatenate([blocks[:, :, :-1], blocks[:, :, 1:]], axis=3).reshape(
        2, count, nseg, radix, radix
    )
    merged = jnp.concatenate([frames[0], frames[1]], axis=-1)
    spectrum = forward_dft(merged, forward_tables)
    shaped = merged_times(spectrum, response)
    outcome = inverse_upper(shaped, inverse_tables)
    out_re = outcome[..., :radix].reshape(count, -1)[:, :range_len] / nfft
    out_im = outcome[..., radix:].reshape(count, -1)[:, :range_len] / nfft
    filtered = jnp.stack([out_re, out_im]).astype(jnp.bfloat16)
    returned = lax.all_to_all(filtered, "range", split_axis=2, concat_axis=1, tiled=True)
    compressed = returned.reshape(2, chans, pulses, cells_dev)
    snapshots = jnp.take(filtered, cells, axis=2)
    partner = partner_2(snapshots, "chan", 0)
    upper = lax.axis_index("chan") == 0
    series_dev = snapshots.shape[1]
    piece = lax.all_gather(snapshots, "range", axis=1, tiled=True)
    joined = jnp.stack([gram(snapshots, piece), gram(partner, piece)], axis=1)
    own_rows = joined[:, 0]
    cross_rows = joined[:, 1]
    other_rows = partner_2(as_sent(cross_rows), "chan", 0).astype(cross_rows.dtype)
    rows_out = jnp.where(
        upper,
        jnp.concatenate([own_rows, other_rows], axis=2),
        jnp.concatenate([other_rows, own_rows], axis=2),
    )
    covariance = (rows_out / TRAIN).reshape(2, 1, series_dev, -1)
    return (compressed, covariance)


def solution(mesh):
    placed = (P("groups", "chan", None, "range"), P(), P("groups", None))
    return jax.shard_map(
        on_device,
        mesh=mesh,
        in_specs=placed,
        out_specs=(P("groups", "chan", None, "range"), P("groups", "chan", "range", None)),
        check_vma=False,
    )
```

profile of v0, /device:TPU:1, one launch (start us, length us, event | category | flops | bytes accessed | tf_op | source)
XLA Modules:
  0.0 279.0 jit_solution(12653052795058454825)
XLA Ops:
  7.2 3.8 %copy.130 = bf16[2,256,8,128]{3,0,2,1:T(2,128)(2,1)} copy(bf16[2,256,8,128]{3,2,1,0:T(8,128)(2,1)} %param.3) | data formatting | bytes 2097152 | tf_op args[0]
  11.0 6.4 %all-to-all-start = ((bf16[2,2048,128]{2,0,1:T(2,128)(2,1)}), bf16[2,2048,128]{2,0,1:T(2,128)(2,1)S(1)}, u32[]{:S(2)}, u32[]{:S(2)}) async-start(bf16[2,2048,128]{2,0,1:T(2,128)(2,1)} %bitcast), calls=%async_computation | async-start | bytes 2097152 | tf_op jit(solution)/shard_map/all_to_all | solution.py:125
  18.5 0.2 reduce-window.4
  18.9 0.1 fusion.84
  19.0 0.1 fusion.85
  19.2 0.1 multiply_sine_fusion.3
  19.3 0.1 multiply_sine_fusion.2
  19.5 0.4 fusion.60
  19.9 0.1 multiply_subtract_fusion.3
  20.1 0.3 fusion.40
  20.4 0.1 multiply_sine_fusion.1
  20.5 0.1 multiply_sine_fusion
  20.8 21.2 %all-to-all-done = bf16[2,2048,128]{2,0,1:T(2,128)(2,1)S(1)} async-done(((bf16[2,2048,128]{2,0,1:T(2,128)(2,1)}), bf16[2,2048,128]{2,0,1:T(2,128)(2,1)S(1)}, u32[]{:S(2)}, u32[]{:S(2)}) %all-to-all-start) | async-done | bytes 1048608 | tf_op jit(solution)/shard_map/all_to_all | solution.py:125
  42.0 0.1 copy.131
  42.1 0.7 copy.132
  42.8 0.3 pad.9
  43.1 0.7 fusion.95
  43.8 3.7 %fusion.12 = (f32[1,256,1,4096]{1,3,2,0:T(8,128)}, f32[1,256,1,4096]{1,3,2,0:T(8,128)}) fusion(f32[2,256,1,2048]{1,3,2,0:T(8,128)S(1)} %get-tuple-element.26, f32[2,256,1,2048]{1,3,2,0:T(8,128)S(1)} %get-tuple-element.27), kind=kLoop, calls=%fused_computation.26 | loop fusion | flops 2097152 | bytes 16777216 | tf_op jit(solution)/shard_map/concatenate | solution.py:130
  47.5 9.1 %copy.133 = f32[256,1,64,64]{3,2,0,1:T(8,128)} copy(f32[256,1,64,64]{0,3,2,1:T(8,128)} %bitcast.180) | data formatting | bytes 8388608 | tf_op jit(solution)/shard_map/squeeze | solution.py:133
  56.7 9.1 %copy.134 = f32[256,1,64,64]{3,2,0,1:T(8,128)} copy(f32[256,1,64,64]{0,3,2,1:T(8,128)} %bitcast.179) | data formatting | bytes 8388608 | tf_op jit(solution)/shard_map/squeeze | solution.py:133
  65.8 20.8 %convolution_bitcast_fusion = f32[256,1,2,64,128]{4,3,2,0,1:T(8,128)} fusion(f32[256,1,64,64]{3,2,0,1:T(8,128)} %copy.134, f32[256,1,64,64]{3,2,0,1:T(8,128)} %copy.133, f32[1,64,64]{2,1,0:T(8,128)S(1)} %get-tuple-element.38, f32[1,64,64]{2,1,0:T(8,128)S(1)} %get-tuple-element.39), kind=kOutput, calls=%fused_computation.1 | convolution fusion | flops 3223330816 | bytes 25198592 | tf_op jit(solution)/shard_map/ckn,...nr->...ckr/dot_general | solution.py:68
  86.6 19.7 %multiply_subtract_fusion = (f32[256,1,64,64]{3,2,0,1:T(8,128)}, f32[256,1,64,64]{3,2,0,1:T(8,128)}) fusion(f32[64,64]{1,0:T(8,128)S(1)} %copy.138, f32[64,64]{1,0:T(8,128)S(1)} %copy.137, f32[256,1,2,64,128]{4,3,2,0,1:T(8,128)} %convolution_bitcast_fusion), kind=kLoop, calls=%fused_computation.25 | loop fusion | flops 8388608 | bytes 25198592 | tf_op jit(solution)/shard_map/sub | solution.py:62
  106.3 11.9 %maximum_bitcast_fusion.2 = f32[256,64,128]{2,1,0:T(8,128)} fusion(f32[256,1,64,64]{3,2,0,1:T(8,128)} %get-tuple-element.17, f32[256,1,64,64]{3,2,0,1:T(8,128)} %get-tuple-element.16), kind=kLoop, calls=%fused_computation.13 | loop fusion | flops 2097152 | bytes 16777216 | tf_op jit(solution)/shard_map/reshape.22
  118.2 16.0 %fusion.13 = f32[256,1,64,128]{0,3,2,1:T(8,128)S(1)} fusion(f32[256,64,128]{2,1,0:T(8,128)} %maximum_bitcast_fusion.2, f32[64,64]{0,1:T(8,128)S(1)} %get-tuple-element.41, f32[64,64]{0,1:T(8,128)S(1)} %fusion.84, f32[64,64]{0,1:T(8,128)S(1)} %get-tuple-element.40), kind=kOutput, calls=%fused_computation.35 | convolution fusion | flops 3221274624 | bytes 16826368 | tf_op jit(solution)/shard_map/...km,mj->...kj/dot_general | solution.py:76
  134.2 1.9 multiply_subtract_fusion.2
  136.1 8.5 %fusion.16 = f32[256,1,64,128]{0,3,2,1:T(8,128)S(1)} fusion(f32[256,1,64,64]{0,3,2,1:T(8,128)S(1)} %get-tuple-element.21, f32[256,1,64,64]{0,3,2,1:T(8,128)S(1)} %get-tuple-element.20, f32[64,64]{0,1:T(8,128)S(1)} %get-tuple-element.43, f32[64,64]{0,1:T(8,128)S(1)} %fusion.85, f32[64,64]{0,1:T(8,128)S(1)} %get-tuple-element.42), kind=kOutput, calls=%fused_computation.37 | convolution fusion | flops 3223371776 | bytes 16826368 | tf_op jit(solution)/shard_map/...km,mj->...kj/dot_general | solution.py:76
  144.6 1.5 multiply_subtract_fusion.1
  146.1 4.0 %maximum_bitcast_fusion.5 = f32[256,64,128,1]{0,2,1,3:T(8,128)} fusion(f32[256,1,64,64]{0,3,2,1:T(8,128)S(1)} %get-tuple-element.19, f32[256,1,64,64]{0,3,2,1:T(8,128)S(1)} %get-tuple-element.18), kind=kLoop, calls=%fused_computation.18 | loop fusion | flops 2097152 | bytes 16777216 | tf_op jit(solution)/shard_map/reshape.38
  150.1 8.7 %copy.165 = f32[256,64,128,1]{2,1,3,0:T(8,128)} copy(f32[256,64,128,1]{0,2,1,3:T(8,128)} %maximum_bitcast_fusion.5) | data formatting | bytes 16777216 | tf_op jit(solution)/shard_map/reshape.38
  158.8 12.3 %convolution_bitcast_fusion.1 = f32[256,1,2,32,128]{4,3,2,0,1:T(8,128)} fusion(f32[256,64,128,1]{2,1,3,0:T(8,128)} %copy.165, f32[1,64,64]{2,1,0:T(8,128)S(1)} %get-tuple-element.44, f32[1,64,64]{2,1,0:T(8,128)S(1)} %get-tuple-element.45), kind=kOutput, calls=%fused_computation.36 | convolution fusion | flops 1610616832 | bytes 16809984 | tf_op jit(solution)/shard_map/ckn,...nr->...ckr/dot_general | solution.py:68
  171.2 11.4 %slice_subtract_fusion = (f32[256,1,1,32,64]{4,3,2,0,1:T(8,128)}, f32[256,1,1,32,64]{4,3,2,0,1:T(8,128)}) fusion(f32[256,1,2,32,128]{4,3,2,0,1:T(8,128)} %convolution_bitcast_fusion.1), kind=kLoop, calls=%fused_computation.28 | loop fusion | flops 1048576 | bytes 12582912 | tf_op jit(solution)/shard_map/sub | solution.py:70
  182.5 3.5 %copy.148 = f32[256,1,1,32,64]{0,4,3,2,1:T(8,128)S(1)} copy(f32[256,1,1,32,64]{4,3,2,0,1:T(8,128)} %get-tuple-element.22) | data formatting | bytes 4194304 | tf_op jit(solution)/shard_map/sub | solution.py:70
  186.2 0.8 copy.152
  187.0 3.6 %copy.150 = f32[256,1,1,32,64]{0,4,3,2,1:T(8,128)S(1)} copy(f32[256,1,1,32,64]{4,3,2,0,1:T(8,128)} %get-tuple-element.23) | data formatting | bytes 4194304 | tf_op jit(solution)/shard_map/add | solution.py:71
  190.6 0.8 copy.153
  191.5 3.4 %pad_maximum_fusion.2 = bf16[2,256,1024]{1,0,2:T(2,128)(2,1)} fusion(bf16[1,256,1024]{1,0,2:T(2,128)(2,1)S(1)} %copy.153, bf16[1,256,1024]{1,0,2:T(2,128)(2,1)S(1)} %copy.152), kind=kLoop, calls=%fused_computation.54 | loop fusion | flops 2097152 | bytes 2097152 | tf_op jit(solution)/shard_map/stack | solution.py:139
  194.9 2.1 gather_fusion
  197.0 0.9 fusion.39
  197.9 2.2 collective-permute-start
  200.1 4.2 %all-to-all-start.1 = ((bf16[2,256,1024]{1,0,2:T(2,128)(2,1)}), bf16[2,256,1024]{1,0,2:T(2,128)(2,1)}, u32[]{:S(2)}, u32[]{:S(2)}) async-start(bf16[2,256,1024]{1,0,2:T(2,128)(2,1)} %pad_maximum_fusion.2), calls=%async_computation.1 | async-start | bytes 2097152 | tf_op jit(solution)/shard_map/all_to_all | solution.py:140
  204.3 0.2 fusion.98
  204.5 0.1 copy.160
  204.7 0.1 copy.159
  204.8 43.3 %all-gather.2.cloned.1.call-done = bf16[2,2048,128]{1,0,2:T(2,128)(2,1)} async-done(((bf16[2,256,128]{1,0,2:T(2,128)(2,1)}), bf16[2,2048,128]{1,0,2:T(2,128)(2,1)}) %all-gather.2.cloned.1.call-update) | async-done | bytes 1048592 | tf_op jit(solution)/shard_map/all_gather | solution.py:146
  248.1 4.2 %fusion.96 = (bf16[1,2048,128]{1,0,2:T(2,128)(2,1)}, bf16[1,2048,128]{1,0,2:T(2,128)(2,1)S(1)}) fusion(bf16[2,2048,128]{1,0,2:T(2,128)(2,1)} %all-gather.2.cloned.1.call-done), kind=kLoop, calls=%fused_computation.165 | loop fusion | bytes 2097152 | tf_op jit(solution)/shard_map/slice | solution.py:100
  252.3 0.8 copy.158
  253.1 0.4 fusion.29
  253.6 2.4 copy.156
  256.0 0.4 fusion.22
  256.4 0.4 fusion.27
  256.9 0.4 fusion.21
  257.3 1.5 pad_maximum_fusion.1
  258.8 2.2 collective-permute-start.1
  261.0 0.2 fusion.97
  261.2 0.1 copy.155
  261.4 0.1 copy.157
  261.5 3.6 %copy.154 = bf16[2,8,256,128]{3,2,1,0:T(8,128)(2,1)} copy(bf16[2,8,256,128]{2,0,3,1:T(2,128)(2,1)} %bitcast.37) | data formatting | bytes 2097152 | tf_op jit(solution)/shard_map/all_to_all | solution.py:140
  265.2 0.4 fusion.37
  265.6 0.4 fusion.18
  266.0 0.4 fusion.35
  266.5 0.4 fusion.17
  266.9 0.5 maximum_bitcast_fusion.6
  267.4 0.5 bitcast_convert_fusion
  268.0 4.0 %fusion.9 = f32[2,1,256,4096]{3,2,1,0:T(8,128)} fusion(f32[2,1,256,2048]{3,2,0,1:T(8,128)S(1)} %bitcast_convert_fusion, f32[2,1,256,2048]{3,2,0,1:T(8,128)S(1)} %maximum_bitcast_fusion.6, pred[]{:T(512)S(6)} %eq.19), kind=kLoop, calls=%fused_computation.21 | loop fusion | flops 8388608 | bytes 16777216
  (32 shorter events, 1.5 us)
Async XLA Ops:
  7.2 10.9 %copy-start.1 = (f32[2,2049]{1,0:T(2,128)S(1)}, f32[2,2049]{1,0:T(2,128)}, u32[]{:S(2)}) copy-start(f32[2,2049]{1,0:T(2,128)} %param.4) | copy-start | bytes 49180
  7.2 11.3 %copy-start.2 = (s32[2,8]{1,0:T(2,128)S(1)}, s32[2,8]{1,0:T(2,128)}, u32[]{:S(2)}) copy-start(s32[2,8]{1,0:T(2,128)} %param.5) | copy-start | bytes 196
  11.0 31.0 %all-to-all-start = ((bf16[2,2048,128]{2,0,1:T(2,128)(2,1)}), bf16[2,2048,128]{2,0,1:T(2,128)(2,1)S(1)}, u32[]{:S(2)}, u32[]{:S(2)}) async-start(bf16[2,2048,128]{2,0,1:T(2,128)(2,1)} %bitcast), calls=%async_computation | async-start | bytes 2097152 | tf_op jit(solution)/shard_map/all_to_all | solution.py:125
  17.4 230.7 %all-gather.2.cloned.1.call-start = ((), (), s32[]{:S(2)}) async-start(), calls=%async_computation.2 | async-start | bytes 1179648 | tf_op jit(solution)/shard_map/all_gather | solution.py:146
  197.9 6.4 %collective-permute-start = (bf16[2,256,128]{1,0,2:T(2,128)(2,1)}, bf16[2,256,128]{1,0,2:T(2,128)(2,1)S(1)}, u32[]{:S(2)}, u32[]{:S(2)}) collective-permute-start(bf16[2,256,128]{1,0,2:T(2,128)(2,1)} %fusion.39), channel_id=1, source_target_pairs={{0,1},{1,0},{2,3},{3,2},{4,5},{5,4},{6,7},{7,6},{8,9},{9,8},{10,11... | collective-permute-start | bytes 393224 | tf_op jit(solution)/shard_map/ppermute | solution.py:14
  200.1 61.4 %all-to-all-start.1 = ((bf16[2,256,1024]{1,0,2:T(2,128)(2,1)}), bf16[2,256,1024]{1,0,2:T(2,128)(2,1)}, u32[]{:S(2)}, u32[]{:S(2)}) async-start(bf16[2,256,1024]{1,0,2:T(2,128)(2,1)} %pad_maximum_fusion.2), calls=%async_computation.1 | async-start | bytes 2097152 | tf_op jit(solution)/shard_map/all_to_all | solution.py:140
  256.9 4.2 %copy-start = (bf16[2,256,128]{1,0,2:T(2,128)(2,1)S(1)}, bf16[2,256,128]{1,0,2:T(2,128)(2,1)}, u32[]{:S(2)}) copy-start(bf16[2,256,128]{1,0,2:T(2,128)(2,1)} %fusion.39) | copy-start | bytes 393220
  258.8 8.6 %collective-permute-start.1 = (bf16[2,256,2048]{2,1,0:T(8,128)(2,1)}, bf16[2,256,2048]{2,1,0:T(8,128)(2,1)S(1)}, u32[]{:S(2)}, u32[]{:S(2)}) collective-permute-start(bf16[2,256,2048]{2,1,0:T(8,128)(2,1)} %pad_maximum_fusion.1), channel_id=1, source_target_pairs={{0,1},{1,0},{2,3},{3,2},{4,5},{5,4},{6,7},{7,6},{8,9},{9,8},{10,11... | collective-permute-start | bytes 6291464 | tf_op jit(solution)/shard_map/ppermute | solution.py:14
Sparse Core Ops, SparseCore 0:
  198.0 50.0 all-gather.1
where the time goes:
time: 284 us; the launch traced here: 279 us
  other arithmetic  66.9 us (24%)
  waiting for transfers between devices  64.5 us (23%)
  matrix products  61.9 us (22%)
  local copies, waits for them, and re-layouts  56 us (20%)
  starting transfers between devices  15 us (5%)
  between operations  14.6 us (5%)
    all_gather x1, waiting for transfers between devices, on_device(): piece = lax.all_gather(snapshots, 'range', axis=1, tiled=True)  43.3 us
    dot_general x3, matrix products, left_section(): jnp.einsum('ckn,...nr->...ckr', stacked, values, precision=lax.Precision....  33.6 us
    dot_general x3, matrix products, right_section(): jnp.einsum('...km,mj->...kj', values, block, precision=lax.Precision.HIGH...  24.8 us
    sub x4, other arithmetic, merged_times(): first_re * second_re - first_im * second_im  23.2 us
    all_to_all x1, waiting for transfers between devices, on_device(): lax.all_to_all(local, 'range', split_axis=1, concat_axis=2, tiled=True)  21.2 us
    squeeze x2, local copies, waits for them, and re-layouts, on_device(): merged = jnp.concatenate([frames[0], frames[1]], axis=-1)  18.2 us
    another operation x3, other arithmetic  16.1 us
    sub x1, other arithmetic, left_section(): real_part = mixed[..., 0, :, :half] - mixed[..., 1, :, half:]  11.4 us
  transfers between devices with their start and end apart: 5, of which 2 were waited for; matrix products, arithmetic and copies ran while one was open for 7% of the time, Pallas kernels for 0%

commit v1 on v0

--- a/solution.py
+++ b/solution.py
@@ -137,7 +137,15 @@
     out_re = outcome[..., :radix].reshape(count, -1)[:, :range_len] / nfft
     out_im = outcome[..., radix:].reshape(count, -1)[:, :range_len] / nfft
     filtered = jnp.stack([out_re, out_im]).astype(jnp.bfloat16)
-    returned = lax.all_to_all(filtered, "range", split_axis=2, concat_axis=1, tiled=True)
+    ways, here = (lax.axis_size("range"), lax.axis_index("range"))
+    width = filtered.shape[2] // ways
+    turned = jnp.roll(filtered, -here * width, axis=2)
+    got = [lax.slice_in_dim(turned, 0, width, axis=2)]
+    for far in range(1, ways):
+        sent = lax.slice_in_dim(turned, far * width, (far + 1) * width, axis=2)
+        got.append(lax.ppermute(sent, "range", [(d, (d + far) % ways) for d in range(ways)]))
+    line = jnp.concatenate(got[::-1], axis=1)
+    returned = jnp.roll(line, (here + 1) * got[0].shape[1], axis=1)
     compressed = returned.reshape(2, chans, pulses, cells_dev)
     snapshots = jnp.take(filtered, cells, axis=2)
     partner = partner_2(snapshots, "chan", 0)

time: 284 us -> 294 us (1.035)
  local copies, waits for them, and re-layouts: 56 us -> 69.1 us
  waiting for transfers between devices: 64.5 us -> 52.9 us
  other arithmetic: 66.9 us -> 75.4 us
    all_gather x1, waiting for transfers between devices: 43.3 us -> 15.4 us  [on_device(): piece = lax.all_gather(snapshots, 'range', axis=1, tiled=True)]
    ppermute x0 -> x7, waiting for transfers between devices: none -> 16.4 us  [on_device(): lax.ppermute(sent, 'range', [(d, (d + far) % ways) for d in range(ways)])]
    unnamed x7 -> x28, local copies, waits for them, and re-layouts: 3.85 us -> 15.1 us
    another operation x3, other arithmetic: 3.57 us -> 10.5 us  [on_device(): filtered = jnp.stack([out_re, out_im]).astype(jnp.bfloat16)]
    ppermute x0 -> x7, starting transfers between devices: none -> 6.01 us  [on_device(): lax.ppermute(sent, 'range', [(d, (d + far) % ways) for d in range(ways)])]
    all_to_all x1 -> x0, starting transfers between devices: 4.24 us -> none  [on_device(): lax.all_to_all(filtered, 'range', split_axis=2, concat_axis=1, tiled=True)]
    dynamic_slice x0 -> x2, local copies, waits for them, and re-layouts: none -> 4.04 us  [on_device(): returned = jnp.roll(line, (here + 1) * got[0].shape[1], axis=1)]
    all_to_all x1 -> x0, local copies, waits for them, and re-layouts: 3.64 us -> none  [on_device(): lax.all_to_all(filtered, 'range', split_axis=2, concat_axis=1, tiled=True)]
  transfers between devices with their start and end apart: 5 -> 11, of which waited for: 2 -> 6; matrix products, arithmetic and copies ran while one was open for 7% -> 8% of each run, Pallas kernels for 0% -> 0%
where the time goes in v1:
time: 294 us; the launch traced here: 289 us
  other arithmetic  75.4 us (26%)
  local copies, waits for them, and re-layouts  69.1 us (24%)
  matrix products  61.9 us (21%)
  waiting for transfers between devices  52.9 us (18%)
  starting transfers between devices  15.1 us (5%)
  between operations  15 us (5%)
    dot_general x3, matrix products, left_section(): jnp.einsum('ckn,...nr->...ckr', stacked, values, precision=lax.Precision....  33.6 us
    dot_general x3, matrix products, right_section(): jnp.einsum('...km,mj->...kj', values, block, precision=lax.Precision.HIGH...  24.8 us
    sub x4, other arithmetic, merged_times(): first_re * second_re - first_im * second_im  23.1 us
    all_to_all x1, waiting for transfers between devices, on_device(): lax.all_to_all(local, 'range', split_axis=1, concat_axis=2, tiled=True)  21.2 us
    squeeze x2, local copies, waits for them, and re-layouts, on_device(): merged = jnp.concatenate([frames[0], frames[1]], axis=-1)  18.3 us
    ppermute x7, waiting for transfers between devices, on_device(): lax.ppermute(sent, 'range', [(d, (d + far) % ways) for d in range(ways)])  16.4 us
    another operation x3, other arithmetic  16.1 us
    all_gather x1, waiting for transfers between devices, on_device(): piece = lax.all_gather(snapshots, 'range', axis=1, tiled=True)  15.4 us
  transfers between devices with their start and end apart: 11, of which 6 were waited for; matrix products, arithmetic and copies ran while one was open for 8% of the time, Pallas kernels for 0%

profile of v1, /device:TPU:1, one launch (start us, length us, event | category | flops | bytes accessed | tf_op | source)
XLA Modules:
  0.0 289.5 jit_solution(10814845574702148751)
XLA Ops:
  7.2 3.8 %copy.128 = bf16[2,256,8,128]{3,0,2,1:T(2,128)(2,1)} copy(bf16[2,256,8,128]{3,2,1,0:T(8,128)(2,1)} %param.3) | data formatting | bytes 2097152 | tf_op args[0]
  11.0 6.4 %all-to-all-start = ((bf16[2,2048,128]{2,0,1:T(2,128)(2,1)}), bf16[2,2048,128]{2,0,1:T(2,128)(2,1)S(1)}, u32[]{:S(2)}, u32[]{:S(2)}) async-start(bf16[2,2048,128]{2,0,1:T(2,128)(2,1)} %bitcast), calls=%async_computation | async-start | bytes 2097152 | tf_op jit(solution)/shard_map/all_to_all | solution.py:125
  20.8 21.2 %all-to-all-done = bf16[2,2048,128]{2,0,1:T(2,128)(2,1)S(1)} async-done(((bf16[2,2048,128]{2,0,1:T(2,128)(2,1)}), bf16[2,2048,128]{2,0,1:T(2,128)(2,1)S(1)}, u32[]{:S(2)}, u32[]{:S(2)}) %all-to-all-start) | async-done | bytes 1048608 | tf_op jit(solution)/shard_map/all_to_all | solution.py:125
  42.1 0.7 copy.130
  43.1 0.7 fusion.98
  43.9 3.7 %fusion.12 = (f32[1,256,1,4096]{1,3,2,0:T(8,128)}, f32[1,256,1,4096]{1,3,2,0:T(8,128)}) fusion(f32[2,256,1,2048]{1,3,2,0:T(8,128)S(1)} %get-tuple-element.26, f32[2,256,1,2048]{1,3,2,0:T(8,128)S(1)} %get-tuple-element.27), kind=kLoop, calls=%fused_computation.26 | loop fusion | flops 2097152 | bytes 16777216 | tf_op jit(solution)/shard_map/concatenate | solution.py:130
  47.6 9.2 %copy.131 = f32[256,1,64,64]{3,2,0,1:T(8,128)} copy(f32[256,1,64,64]{0,3,2,1:T(8,128)} %bitcast.177) | data formatting | bytes 8388608 | tf_op jit(solution)/shard_map/squeeze | solution.py:133
  56.7 9.1 %copy.132 = f32[256,1,64,64]{3,2,0,1:T(8,128)} copy(f32[256,1,64,64]{0,3,2,1:T(8,128)} %bitcast.176) | data formatting | bytes 8388608 | tf_op jit(solution)/shard_map/squeeze | solution.py:133
  65.8 20.8 %convolution_bitcast_fusion = f32[256,1,2,64,128]{4,3,2,0,1:T(8,128)} fusion(f32[256,1,64,64]{3,2,0,1:T(8,128)} %copy.132, f32[256,1,64,64]{3,2,0,1:T(8,128)} %copy.131, f32[1,64,64]{2,1,0:T(8,128)S(1)} %get-tuple-element.47, f32[1,64,64]{2,1,0:T(8,128)S(1)} %get-tuple-element.48), kind=kOutput, calls=%fused_computation.1 | convolution fusion | flops 3223330816 | bytes 25198592 | tf_op jit(solution)/shard_map/ckn,...nr->...ckr/dot_general | solution.py:68
  86.6 19.9 %multiply_subtract_fusion = (f32[256,1,64,64]{3,2,0,1:T(8,128)}, f32[256,1,64,64]{3,2,0,1:T(8,128)}) fusion(f32[64,64]{1,0:T(8,128)S(1)} %copy.136, f32[64,64]{1,0:T(8,128)S(1)} %copy.135, f32[256,1,2,64,128]{4,3,2,0,1:T(8,128)} %convolution_bitcast_fusion), kind=kLoop, calls=%fused_computation.25 | loop fusion | flops 8388608 | bytes 25198592 | tf_op jit(solution)/shard_map/sub | solution.py:62
  106.5 11.9 %maximum_bitcast_fusion.2 = f32[256,64,128]{2,1,0:T(8,128)} fusion(f32[256,1,64,64]{3,2,0,1:T(8,128)} %get-tuple-element.17, f32[256,1,64,64]{3,2,0,1:T(8,128)} %get-tuple-element.16), kind=kLoop, calls=%fused_computation.13 | loop fusion | flops 2097152 | bytes 16777216 | tf_op jit(solution)/shard_map/reshape.22
  118.5 16.0 %fusion.13 = f32[256,1,64,128]{0,3,2,1:T(8,128)S(1)} fusion(f32[256,64,128]{2,1,0:T(8,128)} %maximum_bitcast_fusion.2, f32[64,64]{0,1:T(8,128)S(1)} %get-tuple-element.50, f32[64,64]{0,1:T(8,128)S(1)} %fusion.87, f32[64,64]{0,1:T(8,128)S(1)} %get-tuple-element.49), kind=kOutput, calls=%fused_computation.35 | convolution fusion | flops 3221274624 | bytes 16826368 | tf_op jit(solution)/shard_map/...km,mj->...kj/dot_general | solution.py:76
  134.5 1.6 multiply_subtract_fusion.2
  136.1 8.5 %fusion.16 = f32[256,1,64,128]{0,3,2,1:T(8,128)S(1)} fusion(f32[256,1,64,64]{0,3,2,1:T(8,128)S(1)} %get-tuple-element.21, f32[256,1,64,64]{0,3,2,1:T(8,128)S(1)} %get-tuple-element.20, f32[64,64]{0,1:T(8,128)S(1)} %get-tuple-element.52, f32[64,64]{0,1:T(8,128)S(1)} %fusion.88, f32[64,64]{0,1:T(8,128)S(1)} %get-tuple-element.51), kind=kOutput, calls=%fused_computation.37 | convolution fusion | flops 3223371776 | bytes 16826368 | tf_op jit(solution)/shard_map/...km,mj->...kj/dot_general | solution.py:76
  144.6 1.5 multiply_subtract_fusion.1
  146.1 4.0 %maximum_bitcast_fusion.5 = f32[256,64,128,1]{0,2,1,3:T(8,128)} fusion(f32[256,1,64,64]{0,3,2,1:T(8,128)S(1)} %get-tuple-element.19, f32[256,1,64,64]{0,3,2,1:T(8,128)S(1)} %get-tuple-element.18), kind=kLoop, calls=%fused_computation.18 | loop fusion | flops 2097152 | bytes 16777216 | tf_op jit(solution)/shard_map/reshape.38
  150.1 8.7 %copy.163 = f32[256,64,128,1]{2,1,3,0:T(8,128)} copy(f32[256,64,128,1]{0,2,1,3:T(8,128)} %maximum_bitcast_fusion.5) | data formatting | bytes 16777216 | tf_op jit(solution)/shard_map/reshape.38
  158.8 12.4 %convolution_bitcast_fusion.1 = f32[256,1,2,32,128]{4,3,2,0,1:T(8,128)} fusion(f32[256,64,128,1]{2,1,3,0:T(8,128)} %copy.163, f32[1,64,64]{2,1,0:T(8,128)S(1)} %get-tuple-element.53, f32[1,64,64]{2,1,0:T(8,128)S(1)} %get-tuple-element.54), kind=kOutput, calls=%fused_computation.36 | convolution fusion | flops 1610616832 | bytes 16809984 | tf_op jit(solution)/shard_map/ckn,...nr->...ckr/dot_general | solution.py:68
  171.2 11.4 %slice_subtract_fusion = (f32[256,1,1,32,64]{4,3,2,0,1:T(8,128)}, f32[256,1,1,32,64]{4,3,2,0,1:T(8,128)}) fusion(f32[256,1,2,32,128]{4,3,2,0,1:T(8,128)} %convolution_bitcast_fusion.1), kind=kLoop, calls=%fused_computation.28 | loop fusion | flops 1048576 | bytes 12582912 | tf_op jit(solution)/shard_map/sub | solution.py:70
  182.6 3.5 %copy.146 = f32[256,1,1,32,64]{0,4,3,2,1:T(8,128)S(1)} copy(f32[256,1,1,32,64]{4,3,2,0,1:T(8,128)} %get-tuple-element.22) | data formatting | bytes 4194304 | tf_op jit(solution)/shard_map/sub | solution.py:70
  186.3 0.8 copy.150
  187.1 3.6 %copy.148 = f32[256,1,1,32,64]{0,4,3,2,1:T(8,128)S(1)} copy(f32[256,1,1,32,64]{4,3,2,0,1:T(8,128)} %get-tuple-element.23) | data formatting | bytes 4194304 | tf_op jit(solution)/shard_map/add | solution.py:71
  190.7 0.8 copy.151
  191.5 10.3 %pad_maximum_fusion.2 = (bf16[2,256,1024]{1,0,2:T(2,128)(2,1)S(1)}, bf16[2,256,1024]{1,0,2:T(2,128)(2,1)S(1)}) fusion(bf16[1,256,1024]{1,0,2:T(2,128)(2,1)S(1)} %copy.151, bf16[1,256,1024]{1,0,2:T(2,128)(2,1)S(1)} %copy.150, s32[]{:T(128)S(6)} %select_n.114), kind=kLoop, calls=%fused_computation.60 | loop fusion | flops 6291456 | bytes 3145732 | tf_op jit(solution)/shard_map/stack | solution.py:139
  201.9 0.9 gather_fusion
  202.8 0.9 fusion.42
  203.7 2.2 collective-permute-start.7
  205.8 0.6 fusion.100
  206.5 1.2 fusion.101
  208.0 2.1 collective-permute-start
  210.1 2.4 collective-permute-start.3
  212.5 1.4 collective-permute-start.4
  214.2 0.7 constant_dynamic-update-slice_fusion.13
  215.0 2.8 collective-permute-done.1
  217.8 0.7 constant_dynamic-update-slice_fusion.12
  218.7 0.7 constant_dynamic-update-slice_fusion.11
  219.4 12.4 %collective-permute-done.3 = bf16[2,256,128]{1,0,2:T(2,128)(2,1)S(1)} collective-permute-done((bf16[2,256,128]{1,0,2:T(2,128)(2,1)S(1)}, bf16[2,256,128]{1,0,2:T(2,128)(2,1)S(1)}, u32[]{:S(2)}, u32[]{:S(2)}) %collective-permute-start.3) | collective-permute-done | bytes 131104 | tf_op jit(solution)/shard_map/ppermute | solution.py:146
  231.8 0.7 constant_dynamic-update-slice_fusion.10
  232.6 1.0 collective-permute-done.4
  233.5 0.7 constant_dynamic-update-slice_fusion.9
  234.6 0.8 constant_dynamic-update-slice_fusion.8
  235.3 0.7 constant_dynamic-update-slice_fusion.7
  236.1 0.7 slice_dynamic-update-slice_fusion
  236.8 0.7 constant_dynamic-update-slice_fusion.6
  237.6 0.7 constant_dynamic-update-slice_fusion.5
  238.3 0.7 constant_dynamic-update-slice_fusion.4
  239.1 0.7 constant_dynamic-update-slice_fusion.3
  239.8 15.4 %all-gather.2.cloned.1.call-done = bf16[2,2048,128]{1,0,2:T(2,128)(2,1)} async-done(((bf16[2,256,128]{1,0,2:T(2,128)(2,1)}), bf16[2,2048,128]{1,0,2:T(2,128)(2,1)}) %all-gather.2.cloned.1.call-update) | async-done | bytes 1048592 | tf_op jit(solution)/shard_map/all_gather | solution.py:154
  255.2 4.5 %fusion.99 = (bf16[1,2048,128]{1,0,2:T(2,128)(2,1)}, bf16[1,2048,128]{1,0,2:T(2,128)(2,1)S(1)}) fusion(bf16[2,2048,128]{1,0,2:T(2,128)(2,1)} %all-gather.2.cloned.1.call-done), kind=kLoop, calls=%fused_computation.189 | loop fusion | bytes 2097152 | tf_op jit(solution)/shard_map/slice | solution.py:100
  259.7 2.4 copy.154
  262.1 0.9 copy.156
  263.8 0.4 fusion.22
  264.3 0.4 fusion.21
  264.7 1.5 pad_maximum_fusion.1
  266.2 0.5 collective-permute-start.8
  266.7 0.7 constant_dynamic-update-slice_fusion.2
  267.5 0.7 constant_dynamic-update-slice_fusion.1
  268.2 0.7 constant_dynamic-update-slice_fusion
  269.0 0.7 slice_dynamic-update-slice_fusion.1
  269.7 1.9 constant_dynamic-slice_fusion
  271.7 2.1 copy.152
  275.5 0.5 maximum_bitcast_fusion.6
  276.0 2.1 bitcast_convert_fusion
  278.1 4.0 %fusion.9 = f32[2,1,256,4096]{3,2,1,0:T(8,128)} fusion(f32[2,1,256,2048]{3,2,0,1:T(8,128)S(1)} %bitcast_convert_fusion, f32[2,1,256,2048]{3,2,0,1:T(8,128)S(1)} %maximum_bitcast_fusion.6, pred[]{:T(512)S(6)} %eq.24), kind=kLoop, calls=%fused_computation.21 | loop fusion | flops 8388608 | bytes 16777216
  (68 shorter events, 7.5 us)
Async XLA Ops:
  7.2 11.0 %copy-start.4 = (f32[2,2049]{1,0:T(2,128)S(1)}, f32[2,2049]{1,0:T(2,128)}, u32[]{:S(2)}) copy-start(f32[2,2049]{1,0:T(2,128)} %param.4) | copy-start | bytes 49180
  7.2 11.3 %copy-start.5 = (s32[2,8]{1,0:T(2,128)S(1)}, s32[2,8]{1,0:T(2,128)}, u32[]{:S(2)}) copy-start(s32[2,8]{1,0:T(2,128)} %param.5) | copy-start | bytes 196
  11.0 31.0 %all-to-all-start = ((bf16[2,2048,128]{2,0,1:T(2,128)(2,1)}), bf16[2,2048,128]{2,0,1:T(2,128)(2,1)S(1)}, u32[]{:S(2)}, u32[]{:S(2)}) async-start(bf16[2,2048,128]{2,0,1:T(2,128)(2,1)} %bitcast), calls=%async_computation | async-start | bytes 2097152 | tf_op jit(solution)/shard_map/all_to_all | solution.py:125
  17.4 237.8 %all-gather.2.cloned.1.call-start = ((), (), s32[]{:S(2)}) async-start(), calls=%async_computation.1 | async-start | bytes 1179648 | tf_op jit(solution)/shard_map/all_gather | solution.py:154
  203.7 8.8 %collective-permute-start.7 = (bf16[2,256,128]{1,0,2:T(2,128)(2,1)}, bf16[2,256,128]{1,0,2:T(2,128)(2,1)S(1)}, u32[]{:S(2)}, u32[]{:S(2)}) collective-permute-start(bf16[2,256,128]{1,0,2:T(2,128)(2,1)} %fusion.42), channel_id=1, source_target_pairs={{0,1},{1,0},{2,3},{3,2},{4,5},{5,4},{6,7},{7,6},{8,9},{9,8},{10,11... | collective-permute-start | bytes 393224 | tf_op jit(solution)/shard_map/ppermute | solution.py:14
  208.0 6.1 %collective-permute-start = (bf16[2,256,128]{1,0,2:T(2,128)(2,1)S(1)}, bf16[2,256,128]{1,0,2:T(2,128)(2,1)S(1)}, u32[]{:S(2)}, u32[]{:S(2)}) collective-permute-start(bf16[2,256,128]{1,0,2:T(2,128)(2,1)S(1)} %get-tuple-element.38), channel_id=1, source_target_pairs={{0,14},{2,0},{4,2},{6,4},{8,6},{10,8},{12,10},{14,12},{1,15},{3,1}... | collective-permute-start | bytes 393224 | tf_op jit(solution)/shard_map/ppermute | solution.py:146
  210.1 7.7 %collective-permute-start.1 = (bf16[2,256,128]{1,0,2:T(2,128)(2,1)S(1)}, bf16[2,256,128]{1,0,2:T(2,128)(2,1)S(1)}, u32[]{:S(2)}, u32[]{:S(2)}) collective-permute-start(bf16[2,256,128]{1,0,2:T(2,128)(2,1)S(1)} %get-tuple-element.37), channel_id=1, source_target_pairs={{0,12},{2,14},{4,0},{6,2},{8,4},{10,6},{12,8},{14,10},{1,13},{3,15... | collective-permute-start | bytes 393224 | tf_op jit(solution)/shard_map/ppermute | solution.py:146
  210.1 8.6 %collective-permute-start.2 = (bf16[2,256,128]{1,0,2:T(2,128)(2,1)S(1)}, bf16[2,256,128]{1,0,2:T(2,128)(2,1)S(1)}, u32[]{:S(2)}, u32[]{:S(2)}) collective-permute-start(bf16[2,256,128]{1,0,2:T(2,128)(2,1)S(1)} %get-tuple-element.36), channel_id=1, source_target_pairs={{0,10},{2,12},{4,14},{6,0},{8,2},{10,4},{12,6},{14,8},{1,11},{3,13... | collective-permute-start | bytes 393224 | tf_op jit(solution)/shard_map/ppermute | solution.py:146
  210.1 21.7 %collective-permute-start.3 = (bf16[2,256,128]{1,0,2:T(2,128)(2,1)S(1)}, bf16[2,256,128]{1,0,2:T(2,128)(2,1)S(1)}, u32[]{:S(2)}, u32[]{:S(2)}) collective-permute-start(bf16[2,256,128]{1,0,2:T(2,128)(2,1)S(1)} %get-tuple-element.35), channel_id=1, source_target_pairs={{0,8},{2,10},{4,12},{6,14},{8,0},{10,2},{12,4},{14,6},{1,9},{3,11}... | collective-permute-start | bytes 393224 | tf_op jit(solution)/shard_map/ppermute | solution.py:146
  212.5 21.0 %collective-permute-start.4 = (bf16[2,256,128]{1,0,2:T(2,128)(2,1)S(1)}, bf16[2,256,128]{1,0,2:T(2,128)(2,1)S(1)}, u32[]{:S(2)}, u32[]{:S(2)}) collective-permute-start(bf16[2,256,128]{1,0,2:T(2,128)(2,1)S(1)} %get-tuple-element.34), channel_id=1, source_target_pairs={{0,6},{2,8},{4,10},{6,12},{8,14},{10,0},{12,2},{14,4},{1,7},{3,9},... | collective-permute-start | bytes 393224 | tf_op jit(solution)/shard_map/ppermute | solution.py:146
  214.1 20.4 %collective-permute-start.5 = (bf16[2,256,128]{1,0,2:T(2,128)(2,1)S(1)}, bf16[2,256,128]{1,0,2:T(2,128)(2,1)S(1)}, u32[]{:S(2)}, u32[]{:S(2)}) collective-permute-start(bf16[2,256,128]{1,0,2:T(2,128)(2,1)S(1)} %get-tuple-element.33), channel_id=1, source_target_pairs={{0,4},{2,6},{4,8},{6,10},{8,12},{10,14},{12,0},{14,2},{1,5},{3,7},... | collective-permute-start | bytes 393224 | tf_op jit(solution)/shard_map/ppermute | solution.py:146
  217.8 17.6 %collective-permute-start.6 = (bf16[2,256,128]{1,0,2:T(2,128)(2,1)S(1)}, bf16[2,256,128]{1,0,2:T(2,128)(2,1)S(1)}, u32[]{:S(2)}, u32[]{:S(2)}) collective-permute-start(bf16[2,256,128]{1,0,2:T(2,128)(2,1)S(1)} %get-tuple-element.32), channel_id=1, source_target_pairs={{0,2},{2,4},{4,6},{6,8},{8,10},{10,12},{12,14},{14,0},{1,3},{3,5},... | collective-permute-start | bytes 393224 | tf_op jit(solution)/shard_map/ppermute | solution.py:146
  234.6 25.1 %copy-start = (bf16[2,256,128]{1,0,2:T(2,128)(2,1)}, bf16[2,256,128]{1,0,2:T(2,128)(2,1)S(1)}, u32[]{:S(2)}) copy-start(bf16[2,256,128]{1,0,2:T(2,128)(2,1)S(1)} %collective-permute-done.5) | copy-start | bytes 393220
  235.3 24.3 %copy-start.2 = (bf16[2,256,128]{1,0,2:T(2,128)(2,1)}, bf16[2,256,128]{1,0,2:T(2,128)(2,1)S(1)}, u32[]{:S(2)}) copy-start(bf16[2,256,128]{1,0,2:T(2,128)(2,1)S(1)} %collective-permute-done.6) | copy-start | bytes 393220
  264.3 3.2 %copy-start.1 = (bf16[2,256,128]{1,0,2:T(2,128)(2,1)S(1)}, bf16[2,256,128]{1,0,2:T(2,128)(2,1)}, u32[]{:S(2)}) copy-start(bf16[2,256,128]{1,0,2:T(2,128)(2,1)} %copy-done) | copy-start | bytes 393220
  264.3 4.0 %copy-start.3 = (bf16[2,256,128]{1,0,2:T(2,128)(2,1)S(1)}, bf16[2,256,128]{1,0,2:T(2,128)(2,1)}, u32[]{:S(2)}) copy-start(bf16[2,256,128]{1,0,2:T(2,128)(2,1)} %copy-done.2) | copy-start | bytes 393220
  266.2 9.8 %collective-permute-start.8 = (bf16[2,256,2048]{2,1,0:T(8,128)(2,1)}, bf16[2,256,2048]{2,1,0:T(8,128)(2,1)}, u32[]{:S(2)}, u32[]{:S(2)}) collective-permute-start(bf16[2,256,2048]{2,1,0:T(8,128)(2,1)} %pad_maximum_fusion.1), channel_id=1, source_target_pairs={{0,1},{1,0},{2,3},{3,2},{4,5},{5,4},{6,7},{7,6},{8,9},{9,8},{10,11... | collective-permute-start | bytes 6291464 | tf_op jit(solution)/shard_map/ppermute | solution.py:14
Sparse Core Ops, SparseCore 0:
  203.8 51.3 all-gather.1
